TPU v7x, 512 devices: a whole 4x8x8 slice. The times are simulated.
512 devices in a mesh: dp: 128 (over z, y, core), proto: 4 (over x).
Axes of the slice: x: 4, y: 8, z: 8, core: 2. Of those that a mesh axis runs over, the one named last changes fastest.
Arguments:
- teacher_emb: bfloat16 [32768, 128], P('dp'), may hold values from -64 to 64
- student_emb: bfloat16 [32768, 128], P('dp'), may hold values from -64 to 64
- prototypes: float32 [32768, 128], P(('dp', 'proto')), may hold values from -0.125 to 0.125
Outputs:
- grad_prototypes: float32 [32768, 128], P(('dp', 'proto'))
- grad_student: float32 [32768, 128], P('dp')
All inputs are finite; a program needn't handle non-finite values.
Results may differ from a plain program's by a relative error of at most 0.012.
The roundings to bfloat16 on the way count: a program that leaves them out, or rounds other values in their place, can miss the bound.
Values may be sent and summed in bfloat16 or wider, within the bound.
No kernel may reach another device: no remote copies, remote signals or barrier semaphores. Data moves between devices by JAX's collectives and lax.ppermute only.
A program may use at most 64 MiB of HBM per device.

v0:
```python
import math
import jax
import jax.numpy as jnp
from jax import lax
from jax.sharding import PartitionSpec as P

ITERS = 3
teacher_temp = 0.07
student_temp = 0.1


def joined(array, axis, combine):
    everything = jax.tree.map(lambda part: lax.all_gather(part, axis), array)
    first = jax.tree.map(lambda part: part[0], everything)

    def hop(k, so_far):
        return combine(so_far, jax.tree.map(lambda part: part[k], everything))

    return lax.fori_loop(1, lax.axis_size(axis), hop, first)


def contract_rows(left, right):
    return lax.dot_general(
        left, right, (((1,), (1,)), ((), ())), preferred_element_type=jnp.float32
    )


def combine_stats(first, second):
    teacher_top = jnp.maximum(first[0], second[0])
    student_top = jnp.maximum(first[1], second[1])
    total = first[2] * jnp.exp(first[1] - student_top) + second[2] * jnp.exp(
        second[1] - student_top
    )
    return (teacher_top, student_top, total)


def per_device(teacher_emb, student_emb, prototypes):
    copies = lax.all_gather(prototypes.astype(jnp.bfloat16), "dp", axis=0, tiled=True)
    rows_here = teacher_emb.shape[0]
    width = teacher_emb.shape[1]
    block = math.gcd(rows_here, 128)
    count_blocks = rows_here // block

    def teacher_block(emb):
        logits = contract_rows(emb, copies)
        top = jnp.max(logits, axis=1)
        return (jnp.exp((logits - top[:, None]) / teacher_temp), top)

    base_local, teacher_local = lax.map(
        teacher_block, teacher_emb.reshape(count_blocks, block, width)
    )
    base_local = base_local.reshape(rows_here, -1)
    teacher_local = teacher_local.reshape(rows_here)

    def student_stats(emb):
        logits = contract_rows(emb, copies) / student_temp
        top = jnp.max(logits, axis=1)
        return (top, jnp.sum(jnp.exp(logits - top[:, None]), axis=1))

    student_local, total_local = lax.map(
        student_stats, student_emb.reshape(count_blocks, block, width)
    )
    student_local = student_local.reshape(rows_here)
    total_local = total_local.reshape(rows_here)
    teacher_top, student_top, total = joined(
        (teacher_local, student_local, total_local), "proto", combine_stats
    )
    shift = jnp.exp((teacher_local - teacher_top) / teacher_temp)
    row_scale = jnp.ones((rows_here,), jnp.float32)
    col_scale = jnp.ones((base_local.shape[1],), jnp.float32)
    for step in range(ITERS):
        partial_cols = jnp.dot(row_scale * shift, base_local, precision=lax.Precision.HIGHEST)
        col_scale = 1.0 / lax.psum(partial_cols, "dp")
        partial_rows = shift * jnp.dot(base_local, col_scale, precision=lax.Precision.HIGHEST)
        row_scale = 1.0 / lax.psum(partial_rows, "proto")
    row_factor = row_scale * shift
    student_factor = jnp.exp(student_local - student_top) / total

    def gradient_block(items):
        emb, plan, factor, local_top, soft_factor = items
        logits = contract_rows(emb, copies) / student_temp
        probs = jnp.exp(logits - local_top[:, None]) * soft_factor[:, None]
        targets = factor[:, None] * plan * col_scale[None, :]
        grads = (probs - targets).astype(jnp.bfloat16)
        return (grads, jnp.dot(grads, copies, preferred_element_type=jnp.float32) / student_temp)

    grad_logits, student_terms = lax.map(
        gradient_block,
        (
            student_emb.reshape(count_blocks, block, width),
            base_local.reshape(count_blocks, block, -1),
            row_factor.reshape(count_blocks, block),
            student_local.reshape(count_blocks, block),
            student_factor.reshape(count_blocks, block),
        ),
    )
    grad_logits = grad_logits.reshape(rows_here, -1)
    grad_student = lax.psum(student_terms.reshape(rows_here, width), "proto")
    grad_prototypes = lax.psum_scatter(
        lax.dot_general(
            grad_logits, student_emb, (((0,), (0,)), ((), ())), preferred_element_type=jnp.float32
        )
        / student_temp,
        "dp",
        scatter_dimension=0,
        tiled=True,
    )
    return (grad_prototypes, grad_student)


def solution(mesh):
    in_specs = (P("dp", None), P("dp", None), P(("dp", "proto"), None))
    out_specs = (P(("dp", "proto"), None), P("dp", None))
    return jax.shard_map(
        per_device, mesh=mesh, in_specs=in_specs, out_specs=out_specs, check_vma=False
    )
```

profile of v0, /device:TPU:2, one launch (start us, length us, event | category | flops | bytes accessed | tf_op | source)
XLA Modules:
  0.0 1962.5 jit_solution(7701246373878074425)
XLA Ops:
  7.2 1.4 convert_element_type.6
  8.7 90.5 %all-gather.5.cloned.1.call-done = bf16[8192,128]{1,0:T(8,128)(2,1)} async-done(((bf16[64,128]{1,0:T(8,128)(2,1)}), bf16[8192,128]{1,0:T(8,128)(2,1)}) %all-gather.5.cloned.1.call-update) | async-done | bytes 2097168 | tf_op jit(solution)/shard_map/all_gather | solution.py:38
  99.2 6.5 while.55
  99.2 2.4 fusion.65
  102.5 2.4 fusion.65
  105.7 7.8 all-gather.1
  113.6 10.0 while.56
  113.6 2.4 fusion.67
  116.0 2.6 bitcast_dynamic-update-slice_fusion.4
  118.5 2.4 fusion.67
  120.9 2.6 bitcast_dynamic-update-slice_fusion.4
  123.6 9.3 all-gather
  132.9 7.0 all-gather.2
  140.1 7.4 fusion.29
  147.5 490.9 %psum.49 = f32[8192]{0:T(1024)S(1)} all-reduce(f32[8192]{0:T(1024)S(1)} %bitcast.163), channel_id=1, replica_groups=mesh['dp'=128,'proto'=4] {'dp'}, use_global_device_ids=true, to_apply=%region_9.10 | all-reduce | flops 8192 | bytes 65536 | tf_op jit(solution)/shard_map/psum | solution.py:73
  638.4 8.9 fusion.30
  647.3 9.9 psum.50
  657.3 7.4 fusion.31
  664.7 490.9 %psum.51 = f32[8192]{0:T(1024)S(1)} all-reduce(f32[8192]{0:T(1024)S(1)} %bitcast.160), channel_id=1, replica_groups=mesh['dp'=128,'proto'=4] {'dp'}, use_global_device_ids=true, to_apply=%region_11.12 | all-reduce | flops 8192 | bytes 65536 | tf_op jit(solution)/shard_map/psum | solution.py:73
  1155.5 8.9 fusion.32
  1164.5 7.7 psum.52
  1172.2 7.4 fusion.33
  1179.6 491.1 %psum.53 = f32[8192]{0:T(1024)S(1)} all-reduce(f32[8192]{0:T(1024)S(1)} %bitcast.162), channel_id=1, replica_groups=mesh['dp'=128,'proto'=4] {'dp'}, use_global_device_ids=true, to_apply=%region_13.14 | all-reduce | flops 8192 | bytes 65536 | tf_op jit(solution)/shard_map/psum | solution.py:73
  1670.7 9.0 fusion.34
  1679.8 9.7 psum.54
  1689.6 11.7 while.58
  1689.6 5.1 bitcast_dynamic-update-slice_fusion.5
  1695.5 5.0 bitcast_dynamic-update-slice_fusion.5
  1702.0 5.4 convolution_multiply_fusion.3
  1707.4 38.4 %all-reduce.2.cloned.1.call-done = f32[256,128]{1,0:T(8,128)} async-done(((f32[256,128]{1,0:T(8,128)}), f32[256,128]{1,0:T(8,128)}) %all-reduce.2.cloned.1.call-update) | async-done | bytes 131088 | tf_op jit(solution)/shard_map/psum | solution.py:98
  1745.8 208.6 %reduce-scatter.2.cloned.1.call-done = f32[64,128]{1,0:T(8,128)} async-done(((f32[8192,128]{1,0:T(8,128)}), f32[64,128]{1,0:T(8,128)}) %reduce-scatter.2.cloned.1.call-update) | async-done | bytes 32784 | tf_op jit(solution)/shard_map/reduce_scatter | solution.py:99
  1954.4 1.6 copy.62
  (64 shorter events, 4.6 us)
Async XLA Ops:
  7.2 92.1 %all-gather.5.cloned.1.call-start = ((), (), s32[]{:S(2)}) async-start(), calls=%async_computation.1 | async-start | bytes 2113536 | tf_op jit(solution)/shard_map/all_gather | solution.py:38
  8.6 1737.2 %all-reduce.2.cloned.1.call-start = ((), (), s32[]{:S(2)}) async-start(), calls=%async_computation.3 | async-start | bytes 262144 | tf_op jit(solution)/shard_map/psum | solution.py:98
  99.2 14.3 copy-start.2
  1670.7 18.8 copy-start
  1670.7 18.8 copy-start.1
  1701.3 0.7 copy-start.3
  1701.9 252.5 %reduce-scatter.2.cloned.1.call-start = ((), (), s32[]{:S(2)}) async-start(), calls=%async_computation.2 | async-start | bytes 4227072 | tf_op jit(solution)/shard_map/reduce_scatter | solution.py:99
Sparse Core Ops, SparseCore 0:
  11.7 87.4 all-gather.4
  1702.1 43.7 all-reduce.1
  1751.4 202.9 reduce-scatter.1
where the time goes:
time: 1960 us
  blocking collectives  1520 us (78%)
  waiting for transfers between devices  338 us (17%)
  matrix products  75.6 us (4%)
    psum x3, blocking collectives, per_device(): col_scale = 1.0 / lax.psum(partial_cols, 'dp')  1470 us
    reduce_scatter x1, waiting for transfers between devices, per_device(): lax.psum_scatter(lax.dot_general(grad_logits, student_emb, (((0,), (0,)),...  209 us
    all_gather x1, waiting for transfers between devices, per_device(): lax.all_gather(prototypes.astype(jnp.bfloat16), 'dp', axis=0, tiled=True)  90.5 us
  transfers between devices with their start and end apart: 3, of which 3 were waited for; matrix products, arithmetic and copies ran while one was open for 0% of the time, Pallas kernels for 0%

commit v1 on v0

--- a/solution.py
+++ b/solution.py
@@ -7,6 +7,11 @@
 ITERS = 3
 teacher_temp = 0.07
 student_temp = 0.1
+
+
+def summed_here(value, axis):
+    parts = lax.all_gather(value, axis)
+    return jnp.sum(parts, axis=0)
 
 
 def joined(array, axis, combine):
@@ -70,7 +75,7 @@
     col_scale = jnp.ones((base_local.shape[1],), jnp.float32)
     for step in range(ITERS):
         partial_cols = jnp.dot(row_scale * shift, base_local, precision=lax.Precision.HIGHEST)
-        col_scale = 1.0 / lax.psum(partial_cols, "dp")
+        col_scale = 1.0 / summed_here(partial_cols, "dp")
         partial_rows = shift * jnp.dot(base_local, col_scale, precision=lax.Precision.HIGHEST)
         row_scale = 1.0 / lax.psum(partial_rows, "proto")
     row_factor = row_scale * shift

time: 1960 us -> 761 us (0.39)
  blocking collectives: 1520 us -> 50.1 us
  waiting for transfers between devices: 338 us -> 584 us
    psum x3 -> x0, blocking collectives: 1470 us -> none  [per_device(): col_scale = 1.0 / lax.psum(partial_cols, 'dp')]
    all_gather x0 -> x3, waiting for transfers between devices: none -> 243 us  [summed_here(): parts = lax.all_gather(value, axis)]
  transfers between devices with their start and end apart: 3 -> 6, of which waited for: 3 -> 6; matrix products, arithmetic and copies ran while one was open for 0% -> 1% of each run, Pallas kernels for 0% -> 0%
where the time goes in v1:
time: 761 us; the launch traced here: 760 us
  waiting for transfers between devices  584 us (77%)
  matrix products  77.5 us (10%)
  blocking collectives  50.1 us (7%)
  local copies, waits for them, and re-layouts  17.4 us (2%)
  other arithmetic  15.5 us (2%)
  between operations  14.3 us (2%)
    all_gather x3, waiting for transfers between devices, summed_here(): parts = lax.all_gather(value, axis)  243 us
    reduce_scatter x1, waiting for transfers between devices, per_device(): lax.psum_scatter(lax.dot_general(grad_logits, student_emb, (((0,), (0,)),...  208 us
    all_gather x1, waiting for transfers between devices, per_device(): lax.all_gather(prototypes.astype(jnp.bfloat16), 'dp', axis=0, tiled=True)  90.6 us
    psum x1, waiting for transfers between devices, per_device(): grad_student = lax.psum(student_terms.reshape(rows_here, width), 'proto')  42 us
    dot_general x3, matrix products, per_device(): jnp.dot(base_local, col_scale, precision=lax.Precision.HIGHEST)  26.8 us
    psum x3, blocking collectives, per_device(): row_scale = 1.0 / lax.psum(partial_rows, 'proto')  26 us
    all_gather x3, blocking collectives, joined(): everything = jax.tree.map(lambda part: lax.all_gather(part, axis), array)  24.1 us
    dot_general x3, matrix products, per_device(): jnp.dot(row_scale * shift, base_local, precision=lax.Precision.HIGHEST)  24.1 us
  transfers between devices with their start and end apart: 6, of which 6 were waited for; matrix products, arithmetic and copies ran while one was open for 1% of the time, Pallas kernels for 0%

profile of v1, /device:TPU:2, one launch (start us, length us, event | category | flops | bytes accessed | tf_op | source)
XLA Modules:
  0.0 759.9 jit_solution(1050147936345062237)
XLA Ops:
  8.7 90.6 %all-gather.11.cloned.1.call-done = bf16[8192,128]{1,0:T(8,128)(2,1)} async-done(((bf16[64,128]{1,0:T(8,128)(2,1)}), bf16[8192,128]{1,0:T(8,128)(2,1)}) %all-gather.11.cloned.1.call-update) | async-done | bytes 2097168 | tf_op jit(solution)/shard_map/all_gather | solution.py:43
  99.2 6.5 while.55
  99.2 2.4 fusion.65
  105.7 7.8 %all-gather.4 = f32[4,1,256]{2,1,0:T(1,128)S(1)} all-gather(f32[1,1,256]{2,1,0:T(1,128)S(1)} %bitcast.175), channel_id=1, replica_groups=mesh['dp'=128,'proto'=4] {'proto'}, dimensions={0}, use_global_device_ids=true | all-gather | bytes 5120 | tf_op jit(solution)/shard_map/all_gather | solution.py:18
  113.6 10.0 %while.56 = (s32[]{:T(128)}, f32[2,128,8192]{2,1,0:T(8,128)}, f32[2,128]{1,0:T(2,128)S(1)}, bf16[2,128,128]{2,1,0:T(8,128)(2,1)S(1)}, bf16[8192,128]{1,0:T(8,128)(2,1)}, /*index=5*/s32[]{:T(128)}, s32[]{:T(128)}) while((s32[]{:T(128)}, f32[2,128,8192]{2,1,0:T(8,128)}, f32[2,128]{1,0:T(2,128)S(1)}, bf16[2,128,128]{2,1,0:T(8,128)(2,1)S(1)}, ...), condition=%wide.region_2.3_spmd, body=%wide.region_0.2_spmd.sunk | while | flops 271581056 | bytes 14715477 | solution.py:54
  116.0 2.6 bitcast_dynamic-update-slice_fusion.4
  120.9 2.6 bitcast_dynamic-update-slice_fusion.4
  123.6 9.3 %all-gather.3 = f32[4,1,256]{2,1,0:T(1,128)S(1)} all-gather(f32[1,1,256]{2,1,0:T(1,128)S(1)} %bitcast.184), channel_id=1, replica_groups=mesh['dp'=128,'proto'=4] {'proto'}, dimensions={0}, use_global_device_ids=true | all-gather | bytes 5120 | tf_op jit(solution)/shard_map/all_gather | solution.py:18
  132.9 7.0 all-gather.5
  140.1 8.0 %fusion.29 = f32[1,8192]{1,0:T(1,128)} fusion(f32[256,1]{0,1:T(1,128)S(1)} %bitcast.170, f32[256,8192]{1,0:T(8,128)} %bitcast.148), kind=kOutput, calls=%fused_computation.55 | convolution fusion | flops 25165824 | bytes 8422400 | tf_op jit(solution)/shard_map/dot_general | solution.py:77
  148.2 81.1 %all-gather.13.cloned.1.call-done = f32[1048576]{0:T(1024)} async-done(((f32[8192]{0:T(1024)}), f32[1048576]{0:T(1024)}) %all-gather.13.cloned.1.call-update) | async-done | bytes 4194320 | tf_op jit(solution)/shard_map/all_gather | solution.py:13
  229.3 5.0 reshape.50
  234.3 2.4 reduce_sum.36
  236.7 8.9 %fusion.30 = f32[1,256]{1,0:T(1,128)S(1)} fusion(f32[256,8192]{1,0:T(8,128)} %bitcast.149, f32[8192,1]{0,1:T(1,128)S(1)} %bitcast.162), kind=kOutput, calls=%fused_computation.56 | convolution fusion | flops 25165824 | bytes 8422400 | tf_op jit(solution)/shard_map/dot_general | solution.py:79
  245.6 8.8 %psum.28 = f32[256]{0:T(256)S(1)} all-reduce(f32[256]{0:T(256)S(1)} %mul.66), channel_id=1, replica_groups=mesh['dp'=128,'proto'=4] {'proto'}, use_global_device_ids=true, to_apply=%region_10.11 | all-reduce | flops 256 | bytes 2048 | tf_op jit(solution)/shard_map/psum | solution.py:80
  254.4 8.0 %fusion.31 = f32[1,8192]{1,0:T(1,128)} fusion(f32[256,1]{0,1:T(1,128)S(1)} %bitcast.180, f32[256,8192]{1,0:T(8,128)} %bitcast.150), kind=kOutput, calls=%fused_computation.57 | convolution fusion | flops 25165824 | bytes 8422400 | tf_op jit(solution)/shard_map/dot_general | solution.py:77
  262.5 81.3 %all-gather.15.cloned.1.call-done = f32[1048576]{0:T(1024)} async-done(((f32[8192]{0:T(1024)}), f32[1048576]{0:T(1024)}) %all-gather.15.cloned.1.call-update) | async-done | bytes 4194320 | tf_op jit(solution)/shard_map/all_gather | solution.py:13
  343.8 5.0 reshape.51
  351.2 8.9 %fusion.32 = f32[1,256]{1,0:T(1,128)S(1)} fusion(f32[256,8192]{1,0:T(8,128)} %bitcast.151, f32[8192,1]{0,1:T(1,128)S(1)} %bitcast.163), kind=kOutput, calls=%fused_computation.58 | convolution fusion | flops 25165824 | bytes 8422400 | tf_op jit(solution)/shard_map/dot_general | solution.py:79
  360.1 8.6 %psum.29 = f32[256]{0:T(256)S(1)} all-reduce(f32[256]{0:T(256)S(1)} %mul.68), channel_id=1, replica_groups=mesh['dp'=128,'proto'=4] {'proto'}, use_global_device_ids=true, to_apply=%region_12.13 | all-reduce | flops 256 | bytes 2048 | tf_op jit(solution)/shard_map/psum | solution.py:80
  368.8 8.0 %fusion.33 = f32[1,8192]{1,0:T(1,128)} fusion(f32[256,1]{0,1:T(1,128)S(1)} %bitcast.182, f32[256,8192]{1,0:T(8,128)} %bitcast.152), kind=kOutput, calls=%fused_computation.59 | convolution fusion | flops 25165824 | bytes 8422400 | tf_op jit(solution)/shard_map/dot_general | solution.py:77
  377.1 81.0 %all-gather.17.cloned.1.call-done = f32[1048576]{0:T(1024)} async-done(((f32[8192]{0:T(1024)}), f32[1048576]{0:T(1024)}) %all-gather.17.cloned.1.call-update) | async-done | bytes 4194320 | tf_op jit(solution)/shard_map/all_gather | solution.py:13
  458.1 4.9 reshape.52
  463.1 2.4 reduce_sum.38
  465.5 9.0 %fusion.34 = f32[1,256]{1,0:T(1,128)S(1)} fusion(f32[256,8192]{1,0:T(8,128)} %bitcast.153, f32[8192,1]{0,1:T(1,128)S(1)} %bitcast.158), kind=kOutput, calls=%fused_computation.60 | convolution fusion | flops 25165824 | bytes 8422400 | tf_op jit(solution)/shard_map/dot_general | solution.py:79
  474.6 8.6 %psum.30 = f32[256]{0:T(256)S(1)} all-reduce(f32[256]{0:T(256)S(1)} %mul.70), channel_id=1, replica_groups=mesh['dp'=128,'proto'=4] {'proto'}, use_global_device_ids=true, to_apply=%region_14.15 | all-reduce | flops 256 | bytes 2048 | tf_op jit(solution)/shard_map/psum | solution.py:80
  483.2 11.7 %while.58 = (s32[]{:T(128)}, bf16[2,128,8192]{2,1,0:T(8,128)(2,1)}, f32[2,128,128]{2,1,0:T(8,128)S(1)}, bf16[2,128,128]{2,1,0:T(8,128)(2,1)S(1)}, bf16[8192,128]...) while((s32[]{:T(128)}, bf16[2,128,8192]{2,1,0:T(8,128)(2,1)}, ...), condition=%wide.region_16.17_spmd, body=%wide.region_15.16_spmd.sunk | while | flops 544227328 | bytes 14816889 | solution.py:92
  483.3 5.1 bitcast_dynamic-update-slice_fusion.5
  489.1 5.0 bitcast_dynamic-update-slice_fusion.5
  495.6 5.4 convolution_multiply_fusion.3
  501.1 42.0 %all-reduce.2.cloned.1.call-done = f32[256,128]{1,0:T(8,128)} async-done(((f32[256,128]{1,0:T(8,128)}), f32[256,128]{1,0:T(8,128)}) %all-reduce.2.cloned.1.call-update) | async-done | bytes 131088 | tf_op jit(solution)/shard_map/psum | solution.py:103
  543.1 208.4 %reduce-scatter.2.cloned.1.call-done = f32[64,128]{1,0:T(8,128)} async-done(((f32[8192,128]{1,0:T(8,128)}), f32[64,128]{1,0:T(8,128)}) %reduce-scatter.2.cloned.1.call-update) | async-done | bytes 32784 | tf_op jit(solution)/shard_map/reduce_scatter | solution.py:104
  (76 shorter events, 17.5 us)
Async XLA Ops:
  7.2 92.1 %all-gather.11.cloned.1.call-start = ((), (), s32[]{:S(2)}) async-start(), calls=%async_computation.1 | async-start | bytes 2113536 | tf_op jit(solution)/shard_map/all_gather | solution.py:43
  8.6 220.7 %all-gather.13.cloned.1.call-start = ((), (), s32[]{:S(2)}) async-start(), calls=%async_computation.4 | async-start | bytes 4227072 | tf_op jit(solution)/shard_map/all_gather | solution.py:13
  99.2 14.3 %copy-start.2 = (bf16[256,128]{1,0:T(8,128)(2,1)S(1)}, bf16[256,128]{1,0:T(8,128)(2,1)}, u32[]{:S(2)}) copy-start(bf16[256,128]{1,0:T(8,128)(2,1)} %param.11) | copy-start | bytes 196612
  148.2 195.6 %all-gather.15.cloned.1.call-start = ((), (), s32[]{:S(2)}) async-start(), calls=%async_computation.5 | async-start | bytes 4227072 | tf_op jit(solution)/shard_map/all_gather | solution.py:13
  262.5 195.7 %all-gather.17.cloned.1.call-start = ((), (), s32[]{:S(2)}) async-start(), calls=%async_computation.6 | async-start | bytes 4227072 | tf_op jit(solution)/shard_map/all_gather | solution.py:13
  376.8 166.3 %all-reduce.2.cloned.1.call-start = ((), (), s32[]{:S(2)}) async-start(), calls=%async_computation.3 | async-start | bytes 262144 | tf_op jit(solution)/shard_map/psum | solution.py:103
  465.5 17.7 %copy-start = (bf16[8192,128]{1,0:T(8,128)(2,1)S(1)}, bf16[8192,128]{1,0:T(8,128)(2,1)}, u32[]{:S(2)}) copy-start(bf16[8192,128]{1,0:T(8,128)(2,1)} %get-tuple-element.669) | copy-start | bytes 6291460
  465.5 17.7 %copy-start.1 = (bf16[2,128,128]{2,1,0:T(8,128)(2,1)S(1)}, bf16[2,128,128]{2,1,0:T(8,128)(2,1)}, u32[]{:S(2)}) copy-start(bf16[2,128,128]{2,1,0:T(8,128)(2,1)} %get-tuple-element.675) | copy-start | bytes 196612
  494.9 0.7 copy-start.3
  495.6 255.9 %reduce-scatter.2.cloned.1.call-start = ((), (), s32[]{:S(2)}) async-start(), calls=%async_computation.2 | async-start | bytes 4227072 | tf_op jit(solution)/shard_map/reduce_scatter | solution.py:104
Sparse Core Ops, SparseCore 0:
  11.7 87.4 all-gather.10
  148.3 80.9 all-gather.12
  262.6 81.1 all-gather.14
  376.9 81.1 all-gather.16
  495.7 47.3 all-reduce.1
  548.6 202.8 reduce-scatter.1
